TPU v7x, 512 devices: a whole 4x4x16 slice. The times are simulated.
512 devices in a mesh: group: 4 (over z_hi), shard: 16 (over z_lo, y), tensor: 8 (over x, core).
Axes of the slice: x: 4, y: 4, z: 16 (z_hi: 4, z_lo: 4; z = z_hi * 4 + z_lo), core: 2. Of those that a mesh axis runs over, the one named last changes fastest.
Arguments:
- layer_delta: bfloat16 [4, 2, 4, 224, 4864], P('group', None, None, 'shard', 'tensor'), may hold values from -6 to 6
- emb_left: bfloat16 [4, 4, 19200, 64], P('group', None, ('shard', 'tensor')), may hold values from -6 to 6
- emb_right: bfloat16 [4, 64, 896], P('group'), may hold values from -0.75 to 0.75
- layer_weight: float32 [2, 896, 4864], P(None, ('group', 'shard'), 'tensor'), may hold values from -6 to 6
- layer_momentum: float32 [2, 896, 4864], P(None, ('group', 'shard'), 'tensor'), may hold values from -4 to 4
- emb_weight: float32 [76800, 896], P(('group', 'shard', 'tensor')), may hold values from -6 to 6
- emb_momentum: float32 [76800, 896], P(('group', 'shard', 'tensor')), may hold values from -4 to 4
Outputs:
- new_layer_weight: float32 [2, 896, 4864], P(None, ('group', 'shard'), 'tensor')
- new_layer_momentum: float32 [2, 896, 4864], P(None, ('group', 'shard'), 'tensor')
- layer_blocks: bfloat16 [2, 896, 4864], P(None, None, 'tensor')
- new_emb_weight: float32 [76800, 896], P(('group', 'shard', 'tensor'))
- new_emb_momentum: float32 [76800, 896], P(('group', 'shard', 'tensor'))
All inputs are finite; a program needn't handle non-finite values.
Results may differ from a plain program's by a relative error of at most 0.0095.
Values may be sent and summed in bfloat16 or wider, within the bound.
No kernel may reach another device: no remote copies, remote signals or barrier semaphores. Data moves between devices by JAX's collectives and lax.ppermute only.
A program may use at most 64 MiB of HBM per device.

v0:
```python
import jax
import jax.numpy as jnp
from jax import lax
from jax.sharding import PartitionSpec as P

rate_outer = 0.7
beta_outer = 0.9


def on_device(
    layer_delta, emb_left, emb_right, layer_weight, layer_momentum, emb_weight, emb_momentum
):
    groups = lax.axis_size("group")
    summed = lax.psum_scatter(
        layer_delta.astype(jnp.float32).astype(jnp.bfloat16),
        "group",
        scatter_dimension=2,
        tiled=True,
    ).astype(jnp.float32)
    layer_mean = summed.reshape(layer_weight.shape) / groups
    new_layer_momentum = beta_outer * layer_momentum + layer_mean
    new_layer_weight = layer_weight - rate_outer * (layer_mean + beta_outer * new_layer_momentum)
    pieces = new_layer_weight.astype(jnp.bfloat16)
    layer_blocks = lax.all_gather(pieces, ("group", "shard"), axis=1, tiled=True)
    terms = jnp.einsum("qnr,rd->qnd", emb_left[0], emb_right[0], preferred_element_type=jnp.float32)
    total = lax.psum_scatter(
        terms.astype(jnp.bfloat16), "group", scatter_dimension=0, tiled=True
    ).astype(jnp.float32)[0]
    emb_mean = total / groups
    new_emb_momentum = beta_outer * emb_momentum + emb_mean
    new_emb_weight = emb_weight - rate_outer * (emb_mean + beta_outer * new_emb_momentum)
    return (new_layer_weight, new_layer_momentum, layer_blocks, new_emb_weight, new_emb_momentum)


def solution(mesh):
    placed = (
        P("group", None, None, "shard", "tensor"),
        P("group", None, ("shard", "tensor"), None),
        P("group", None, None),
        P(None, ("group", "shard"), "tensor"),
        P(None, ("group", "shard"), "tensor"),
        P(("group", "shard", "tensor"), None),
        P(("group", "shard", "tensor"), None),
    )
    return jax.shard_map(
        on_device,
        mesh=mesh,
        in_specs=placed,
        out_specs=(
            P(None, ("group", "shard"), "tensor"),
            P(None, ("group", "shard"), "tensor"),
            P(None, None, "tensor"),
            P(("group", "shard", "tensor"), None),
            P(("group", "shard", "tensor"), None),
        ),
        check_vma=False,
    )
```

profile of v0, /device:TPU:2, one launch (start us, length us, event | category | flops | bytes accessed | tf_op | source)
XLA Modules:
  0.0 299.9 jit_solution(9431584884943056190)
XLA Ops:
  7.2 0.0 copy-start
  7.2 0.0 copy-start.4
  7.2 0.0 copy-start.3
  7.2 0.0 copy-start.2
  7.2 0.0 copy-start.1
  7.2 0.0 all-reduce.4.cloned.1.call-start
  7.3 1.8 copy.14
  9.0 0.0 all-reduce.4.cloned.1.call-update
  9.1 0.0 reduce-scatter.5.cloned.1.call-start
  9.1 0.0 copy-done
  9.1 2.4 convolution_convert_fusion
  11.5 0.0 reduce-scatter.5.cloned.1.call-update
  11.5 0.0 all-gather.2.cloned.1.call-start
  11.6 1.3 dynamic-slice
  12.9 70.7 %all-reduce.4.cloned.1.call-done = bf16[1,2,4,14,608]{4,1,3,2,0:T(2,128)(2,1)} async-done(((bf16[1,2,4,14,608]{4,1,3,2,0:T(2,128)(2,1)}), bf16[1,2,4,14,608]{4,1,3,2,0:T(2,128)(2,1)}) %all-reduce.4.cloned.1.call-update) | async-done | bytes 136208
  83.6 0.0 copy-done.4
  83.6 0.0 copy-done.3
  83.6 2.2 fusion.6
  85.8 0.0 all-gather.2.cloned.1.call-update
  85.8 59.5 %reduce-scatter.5.cloned.1.call-done = bf16[1,150,896]{2,1,0:T(8,128)(2,1)} async-done(((bf16[4,150,896]{2,1,0:T(8,128)(2,1)}), bf16[1,150,896]{2,1,0:T(8,128)(2,1)}) %reduce-scatter.5.cloned.1.call-update) | async-done | bytes 268816
  145.4 0.0 copy-done.2
  145.4 0.0 copy-done.1
  145.4 2.1 fusion.1
  147.4 138.6 %all-gather.2.cloned.1.call-done = bf16[2,896,608]{2,0,1:T(2,128)(2,1)} async-done(((bf16[2,14,608]{2,0,1:T(2,128)(2,1)}), bf16[2,896,608]{2,0,1:T(2,128)(2,1)}) %all-gather.2.cloned.1.call-update) | async-done | bytes 2179088 | tf_op jit(solution)/shard_map/all_gather | solution.py:24
  286.1 7.3 %copy.15 = bf16[2,896,608]{1,2,0:T(8,128)(2,1)} copy(bf16[2,896,608]{2,0,1:T(2,128)(2,1)} %all-gather.2.cloned.1.call-done) | data formatting | bytes 4358144
Async XLA Ops:
  7.2 2.0 copy-start
  7.2 76.4 %copy-start.4 = (f32[2,14,608]{2,0,1:T(2,128)S(1)}, f32[2,14,608]{2,0,1:T(2,128)}, u32[]{:S(2)}) copy-start(f32[2,14,608]{2,0,1:T(2,128)} %param.11) | copy-start | bytes 204292
  7.2 76.4 %copy-start.3 = (f32[2,14,608]{2,0,1:T(2,128)S(1)}, f32[2,14,608]{2,0,1:T(2,128)}, u32[]{:S(2)}) copy-start(f32[2,14,608]{2,0,1:T(2,128)} %param.10) | copy-start | bytes 204292
  7.2 138.2 %copy-start.2 = (f32[150,896]{1,0:T(8,128)S(1)}, f32[150,896]{1,0:T(8,128)}, u32[]{:S(2)}) copy-start(f32[150,896]{1,0:T(8,128)} %param.13) | copy-start | bytes 1612804
  7.2 138.2 %copy-start.1 = (f32[150,896]{1,0:T(8,128)S(1)}, f32[150,896]{1,0:T(8,128)}, u32[]{:S(2)}) copy-start(f32[150,896]{1,0:T(8,128)} %param.12) | copy-start | bytes 1612804
  7.2 76.4 %all-reduce.4.cloned.1.call-start = ((), (), s32[]{:S(2)}) async-start(), calls=%async_computation.2 | async-start | bytes 286720
  9.1 136.3 %reduce-scatter.5.cloned.1.call-start = ((), (), s32[]{:S(2)}) async-start(), calls=%async_computation.3 | async-start | bytes 1361920
  11.5 274.5 %all-gather.2.cloned.1.call-start = ((), (), s32[]{:S(2)}) async-start(), calls=%async_computation.1 | async-start | bytes 2329600 | tf_op jit(solution)/shard_map/all_gather | solution.py:24
Sparse Core Ops, SparseCore 0:
  11.5 72.0 all-reduce.3
  87.0 58.2 reduce-scatter.4
  148.3 137.6 all-gather.1
where the time goes:
time: 300 us
  waiting for transfers between devices  269 us (90%)
  between operations  13.8 us (5%)
  local copies, waits for them, and re-layouts  10.4 us (3%)
  other arithmetic  4.27 us (1%)
    all_gather x1, waiting for transfers between devices, on_device(): lax.all_gather(pieces, ('group', 'shard'), axis=1, tiled=True)  139 us
    unnamed x5, waiting for transfers between devices  130 us
    unnamed x13, local copies, waits for them, and re-layouts  10.4 us
  transfers between devices with their start and end apart: 3, of which 3 were waited for; matrix products, arithmetic and copies ran while one was open for 3% of the time, Pallas kernels for 0%

commit v1 on v0

--- a/solution.py
+++ b/solution.py
@@ -21,7 +21,10 @@
     new_layer_momentum = beta_outer * layer_momentum + layer_mean
     new_layer_weight = layer_weight - rate_outer * (layer_mean + beta_outer * new_layer_momentum)
     pieces = new_layer_weight.astype(jnp.bfloat16)
-    layer_blocks = lax.all_gather(pieces, ("group", "shard"), axis=1, tiled=True)
+    m_next = lax.axis_size(("group", "shard"))
+    block_now = jnp.stack(m_next * [pieces], axis=0)
+    arr_now = lax.all_to_all(block_now, split_axis=0, concat_axis=0, axis_name=("group", "shard"))
+    layer_blocks = jnp.concatenate(arr_now, axis=1)
     terms = jnp.einsum("qnr,rd->qnd", emb_left[0], emb_right[0], preferred_element_type=jnp.float32)
     total = lax.psum_scatter(
         terms.astype(jnp.bfloat16), "group", scatter_dimension=0, tiled=True

time: 300 us -> 254 us (0.85)
  waiting for transfers between devices: 269 us -> 211 us
  starting transfers between devices: 0.12 us -> 11 us
    all_gather x1 -> x0, waiting for transfers between devices: 139 us -> none  [on_device(): lax.all_gather(pieces, ('group', 'shard'), axis=1, tiled=True)]
    unnamed x5 -> x4, waiting for transfers between devices: 130 us -> 173 us
    all_to_all x0 -> x1, waiting for transfers between devices: none -> 37.4 us  [on_device(): lax.all_to_all(block_now, split_axis=0, concat_axis=0, axis_name=('group'...]
    all_to_all x0 -> x1, starting transfers between devices: none -> 10.9 us  [on_device(): lax.all_to_all(block_now, split_axis=0, concat_axis=0, axis_name=('group'...]
    unnamed x13 -> x9, local copies, waits for them, and re-layouts: 10.4 us -> 8.72 us
  transfers between devices with their start and end apart: 3 -> 3, of which waited for: 3 -> 3; matrix products, arithmetic and copies ran while one was open for 3% -> 2% of each run, Pallas kernels for 0% -> 0%
where the time goes in v1:
time: 254 us
  waiting for transfers between devices  211 us (83%)
  between operations  14.1 us (6%)
  local copies, waits for them, and re-layouts  11.3 us (4%)
  starting transfers between devices  11 us (4%)
  other arithmetic  4.46 us (2%)
    unnamed x4, waiting for transfers between devices  173 us
    all_to_all x1, waiting for transfers between devices, on_device(): lax.all_to_all(block_now, split_axis=0, concat_axis=0, axis_name=('group'...  37.4 us
    all_to_all x1, starting transfers between devices, on_device(): lax.all_to_all(block_now, split_axis=0, concat_axis=0, axis_name=('group'...  10.9 us
    unnamed x9, local copies, waits for them, and re-layouts  8.72 us
  transfers between devices with their start and end apart: 3, of which 3 were waited for; matrix products, arithmetic and copies ran while one was open for 2% of the time, Pallas kernels for 0%

profile of v1, /device:TPU:2, one launch (start us, length us, event | category | flops | bytes accessed | tf_op | source)
XLA Modules:
  0.0 253.9 jit_solution(11012726905625438166)
XLA Ops:
  7.2 0.0 copy-start
  7.2 0.0 all-reduce.4.cloned.1.call-start
  7.2 1.7 copy.16
  8.9 0.0 all-reduce.4.cloned.1.call-update
  9.0 1.3 dynamic-slice
  10.2 73.3 %all-reduce.4.cloned.1.call-done = bf16[1,2,4,14,608]{4,1,3,2,0:T(2,128)(2,1)} async-done(((bf16[1,2,4,14,608]{4,1,3,2,0:T(2,128)(2,1)}), bf16[1,2,4,14,608]{4,1,3,2,0:T(2,128)(2,1)}) %all-reduce.4.cloned.1.call-update) | async-done | bytes 136208
  83.6 2.4 fusion.6
  85.9 2.6 %stack.2 = bf16[64,2,14,608]{3,1,2,0:T(2,128)(2,1)} broadcast(bf16[2,14,608]{2,0,1:T(2,128)(2,1)S(1)} %get-tuple-element.17), dimensions={1,2,3} | broadcast | bytes 2213120 | tf_op jit(solution)/shard_map/stack | solution.py:25
  88.5 10.9 %all-to-all-start = ((bf16[64,2,14,608]{3,1,2,0:T(2,128)(2,1)}), bf16[64,2,14,608]{3,1,2,0:T(2,128)(2,1)S(1)}, u32[]{:S(2)}, u32[]{:S(2)}) async-start(bf16[64,2,14,608]{3,1,2,0:T(2,128)(2,1)} %stack.2), calls=%async_computation | async-start | bytes 4587520 | tf_op jit(solution)/shard_map/all_to_all | solution.py:26
  99.4 0.0 copy-start.1
  99.4 0.0 copy-start.2
  99.4 0.0 reduce-scatter.5.cloned.1.call-start
  99.5 0.0 copy-done
  99.5 2.5 convolution_convert_fusion
  102.0 0.0 reduce-scatter.5.cloned.1.call-update
  102.0 99.8 %reduce-scatter.5.cloned.1.call-done = bf16[1,150,896]{2,1,0:T(8,128)(2,1)} async-done(((bf16[4,150,896]{2,1,0:T(8,128)(2,1)}), bf16[1,150,896]{2,1,0:T(8,128)(2,1)}) %reduce-scatter.5.cloned.1.call-update) | async-done | bytes 268816
  201.8 0.0 copy-done.1
  201.8 0.0 copy-done.2
  201.8 2.1 fusion.1
  203.9 37.4 %all-to-all-done = bf16[64,2,14,608]{3,1,2,0:T(2,128)(2,1)S(1)} async-done(((bf16[64,2,14,608]{3,1,2,0:T(2,128)(2,1)}), bf16[64,2,14,608]{3,1,2,0:T(2,128)(2,1)S(1)}, u32[]{:S(2)}, u32[]{:S(2)}) %all-to-all-start) | async-done | bytes 2179104 | tf_op jit(solution)/shard_map/all_to_all | solution.py:26
  241.3 5.7 %copy.17 = bf16[2,896,608]{1,2,0:T(8,128)(2,1)} copy(bf16[2,896,608]{2,0,1:T(2,128)(2,1)S(1)} %bitcast.32) | data formatting | bytes 4358144
Async XLA Ops:
  7.2 92.3 %copy-start = (bf16[1,4,150,64]{2,3,1,0:T(8,128)(2,1)S(1)}, bf16[1,4,150,64]{2,3,1,0:T(8,128)(2,1)}, u32[]{:S(2)}) copy-start(bf16[1,4,150,64]{2,3,1,0:T(8,128)(2,1)} %param.8) | copy-start | bytes 230404
  7.2 76.4 %all-reduce.4.cloned.1.call-start = ((), (), s32[]{:S(2)}) async-start(), calls=%async_computation.2 | async-start | bytes 286720
  88.5 152.8 %all-to-all-start = ((bf16[64,2,14,608]{3,1,2,0:T(2,128)(2,1)}), bf16[64,2,14,608]{3,1,2,0:T(2,128)(2,1)S(1)}, u32[]{:S(2)}, u32[]{:S(2)}) async-start(bf16[64,2,14,608]{3,1,2,0:T(2,128)(2,1)} %stack.2), calls=%async_computation | async-start | bytes 4587520 | tf_op jit(solution)/shard_map/all_to_all | solution.py:26
  99.4 102.4 %copy-start.1 = (f32[150,896]{1,0:T(8,128)S(1)}, f32[150,896]{1,0:T(8,128)}, u32[]{:S(2)}) copy-start(f32[150,896]{1,0:T(8,128)} %param.12) | copy-start | bytes 1612804
  99.4 102.4 %copy-start.2 = (f32[150,896]{1,0:T(8,128)S(1)}, f32[150,896]{1,0:T(8,128)}, u32[]{:S(2)}) copy-start(f32[150,896]{1,0:T(8,128)} %param.13) | copy-start | bytes 1612804
  99.4 102.4 %reduce-scatter.5.cloned.1.call-start = ((), (), s32[]{:S(2)}) async-start(), calls=%async_computation.3 | async-start | bytes 1361920
Sparse Core Ops, SparseCore 0:
  11.5 72.0 all-reduce.3
  103.7 98.0 reduce-scatter.4
